TPU v7x, 256 devices: a whole 4x4x8 slice. The times are simulated.
256 devices in a mesh: gx: 16 (over y, z_lo), gy: 16 (over x, z_hi, core).
Axes of the slice: x: 4, y: 4, z: 8 (z_hi: 2, z_lo: 4; z = z_hi * 4 + z_lo), core: 2. Of those that a mesh axis runs over, the one named last changes fastest.
Arguments:
- load_vectors: float32 [16, 16, 8, 8, 192], P('gx', 'gy'), may hold values from -45 to 45
- bond_stiffness: bfloat16 [16, 16, 8, 13, 36864], P('gx', 'gy'), may hold values from 0 to 0.0016937256
- intact_words: int32 [16, 16, 8, 13, 64, 4], P('gx', 'gy'), may hold values from 0 to 65535
- block_cols: int32 [16, 16, 8, 13], P('gx', 'gy'), may hold values from 0 to 89, as said below
- self_stiffness: bfloat16 [16, 16, 8, 36864], P('gx', 'gy'), may hold values from -0.01 to 3.01, as said below
- block_inverse: float32 [16, 16, 8, 36864], P('gx', 'gy'), may hold values from -0.01 to 0.61, as said below
- coarse_basis: float32 [16, 16, 16, 8, 192], P('gx', 'gy'), may hold values from -0.3 to 0.3
- coarse_factor: float32 [4096, 4096], P(('gx', 'gy')), may hold values from -0.375 to 0.375
Outputs:
- displacement: float32 [16, 16, 8, 8, 192], P('gx', 'gy')
- residual: float32 [16, 16, 8, 8, 192], P('gx', 'gy')
Inputs may be any that keep to these rules, and one draw needn't show every extreme that they name: `block_cols`: the 13 codes of a block name different blocks among the 26 around it (never the block itself), each |a - 1|, |c - 1|, |w - 1 - z| at most 1. `self_stiffness`: each block, read as a matrix, is symmetric. `block_inverse`: each block, read as a matrix, is symmetric.
All inputs are finite; a program needn't handle non-finite values.
Results may differ from a plain program's by a relative error of at most 0.0055.
Values may be sent and summed in bfloat16 or wider, within the bound.
No kernel may reach another device: no remote copies, remote signals or barrier semaphores. Data moves between devices by JAX's collectives and lax.ppermute only.
A program may use at most 128 MiB of HBM per device.

v0:
```python
import jax
import jax.numpy as jnp
from jax import lax
from jax.sharding import PartitionSpec as P

COMP = 3
PB = 64
DOF = 192
NS = 13
BZ = 8
NLOAD = 8
ITERS = 2
highest = lax.Precision.HIGHEST


def padded_2(x, sides, width):
    for axis, dim in sides:
        size, length = (lax.axis_size(axis), x.shape[dim])
        up = [(i, (i + 1) % size) for i in range(size - 1)]
        down = [(j, i) for i, j in up]
        last = lax.slice_in_dim(x, length - width, length, axis=dim)
        initial = lax.slice_in_dim(x, 0, width, axis=dim)
        before = lax.ppermute(last, axis, up)
        after = lax.ppermute(initial, axis, down)
        x = jnp.concatenate([before, x, after], axis=dim)
    return x


def unpack_bits(packed):
    shifts = jnp.arange(16, dtype=jnp.int32)
    bitset = jnp.right_shift(packed[..., None], shifts) & 1
    return bitset.reshape(packed.shape[:-1] + (packed.shape[-1] * 16,))


def masked_blocks(stiffness, packed):
    intact = unpack_bits(packed).astype(stiffness.dtype)
    leading = stiffness.shape[:-1]
    shaped = stiffness.reshape(leading + (COMP, PB, COMP, PB))
    masked = shaped * intact[..., None, :, None, :]
    return masked.reshape(leading + (DOF, DOF))


def per_device(
    load_vectors,
    bond_stiffness,
    intact_words,
    block_cols,
    self_stiffness,
    block_inverse,
    coarse_basis,
    coarse_factor,
):
    weights = masked_blocks(bond_stiffness[0, 0], intact_words[0, 0])
    row_total = jnp.sum(weights, axis=(1, 3), dtype=jnp.float32)
    column_total = jnp.sum(weights, axis=2, dtype=jnp.float32)
    col_codes = block_cols[0, 0]
    depth_span = BZ + 2
    ghost_count = 9 * depth_span
    selector = (
        jnp.arange(ghost_count, dtype=jnp.int32)[:, None] == col_codes.reshape(-1)[None, :]
    ).astype(jnp.bfloat16)
    self_block = self_stiffness[0, 0].reshape(BZ, DOF, DOF)
    inverse = block_inverse[0, 0].reshape(BZ, DOF, DOF)
    coarse_vecs = coarse_basis[0, 0]

    def smooth_local(field):
        return jnp.einsum("bij,blj->bli", inverse, field, precision=highest)

    def restrict(field):
        restricted = jnp.einsum("kbi,bli->lk", coarse_vecs, field, precision=highest)
        return jnp.dot(restricted, coarse_factor, precision=highest)

    def prolong(summed):
        spread = jnp.einsum("lc,kc->lk", summed, coarse_factor, precision=highest)
        return jnp.einsum("kbi,lk->bli", coarse_vecs, spread, precision=highest)

    def precondition(residual):
        own_part = smooth_local(residual)
        coarse_term = restrict(residual)
        summed = lax.psum(coarse_term, ("gx", "gy"))
        smoothed = own_part + prolong(summed)
        energy = lax.psum(jnp.sum(residual * smoothed, axis=(0, 2)), ("gx", "gy"))
        return (smoothed, energy)

    residual = load_vectors[0, 0]
    solution = jnp.zeros_like(residual)
    smoothed, energy = precondition(residual)
    direction = smoothed
    for iteration in range(ITERS):
        rounded = direction.astype(jnp.bfloat16)
        ghosts = padded_2(rounded[None, None], (("gx", 0), ("gy", 1)), 1)
        padded = jnp.pad(ghosts, ((0, 0), (0, 0), (1, 1), (0, 0), (0, 0))).reshape(
            ghost_count, NLOAD, DOF
        )
        gathered = jnp.take(padded, col_codes, axis=0)
        forward = row_total[:, None, :] * rounded - jnp.einsum(
            "bsij,bslj->bli", weights, gathered, preferred_element_type=jnp.float32
        )
        backward = column_total[:, :, None, :] * gathered - jnp.einsum(
            "bsij,bli->bslj", weights, rounded, preferred_element_type=jnp.float32
        )
        flat_terms = backward.reshape(BZ * NS, NLOAD * DOF)
        high_part = flat_terms.astype(jnp.bfloat16)
        low_part = (flat_terms - high_part.astype(jnp.float32)).astype(jnp.bfloat16)
        apply_spread = jnp.dot(selector, high_part, preferred_element_type=jnp.float32) + jnp.dot(
            selector, low_part, preferred_element_type=jnp.float32
        )
        partial_value = apply_spread.reshape(3, 3, depth_span, NLOAD, DOF)[:, :, 1 : depth_span - 1]
        beside_all = padded_2(partial_value.astype(jnp.bfloat16), (("gx", 0), ("gy", 1)), 1).astype(
            partial_value.dtype
        )
        folded = (
            beside_all[2, 2]
            + beside_all[0, 0]
            + beside_all[0, 2]
            + beside_all[0, 4]
            + beside_all[2, 0]
        )
        folded = folded + beside_all[2, 4] + beside_all[4, 0] + beside_all[4, 2] + beside_all[4, 4]
        diagonal = jnp.einsum(
            "bij,blj->bli", self_block, rounded, preferred_element_type=jnp.float32
        )
        operator_out = diagonal + forward + folded
        curve_sum = lax.psum(jnp.sum(direction * operator_out, axis=(0, 2)), ("gx", "gy"))
        step_scale = (energy / curve_sum)[None, :, None]
        solution = solution + step_scale * direction
        residual = residual - step_scale * operator_out
        if iteration + 1 < ITERS:
            smoothed, new_energy = precondition(residual)
            direction = smoothed + (new_energy / energy)[None, :, None] * direction
            energy = new_energy
    return (solution[None, None], residual[None, None])


def solution(mesh):
    in_specs = (
        P("gx", "gy", None, None, None),
        P("gx", "gy", None, None, None),
        P("gx", "gy", None, None, None, None),
        P("gx", "gy", None, None),
        P("gx", "gy", None, None),
        P("gx", "gy", None, None),
        P("gx", "gy", None, None, None),
        P(("gx", "gy"), None),
    )
    out_specs = (P("gx", "gy", None, None, None), P("gx", "gy", None, None, None))
    return jax.shard_map(
        per_device, mesh=mesh, in_specs=in_specs, out_specs=out_specs, check_vma=False
    )
```

profile of v0, /device:TPU:1, one launch (start us, length us, event | category | flops | bytes accessed | tf_op | source)
XLA Modules:
  0.0 896.7 jit_solution(10883457999654128121)
XLA Ops:
  9.5 2.0 reshape_squeeze.9
  11.5 2.9 fusion.63
  14.4 1.5 fusion.9
  15.9 2.9 copy.45
  18.9 8.8 mul.97
  27.7 34.7 %mul.102 = bf16[8,13,192,192]{3,2,1,0:T(8,128)(2,1)} reshape(bf16[8,13,3,64,3,64]{5,4,3,2,1,0:T(4,128)(2,1)} %mul.97) | data formatting | bytes 15335424 | tf_op jit(solution)/shard_map/mul | solution.py:39
  62.3 16.6 %reshape_squeeze.11 = bf16[8,13,192,192]{3,2,0,1:T(8,128)(2,1)} reshape(bf16[1,1,8,13,36864]{4,2,3,1,0:T(8,128)(2,1)} %param.11) | data formatting | bytes 15335424 | tf_op jit(solution)/shard_map/reshape;squeeze | solution.py:38
  79.0 14.1 %convert_reduce_fusion = (f32[8,13,192]{2,0,1:T(8,128)S(1)}, bf16[8,13,192,192]{3,2,0,1:T(8,128)(2,1)}) fusion(bf16[8,13,192,192]{3,2,0,1:T(8,128)(2,1)} %reshape_squeeze.11, bf16[8,13,192,192]{3,2,1,0:T(8,128)(2,1)} %mul.102), kind=kLoop, calls=%fused_computation.2 | loop fusion | flops 11481600 | bytes 23083008 | tf_op jit(solution)/shard_map/reduce_sum | solution.py:55
  93.1 168.8 %all-reduce.6.cloned.1.call-done = f32[8,4096]{1,0:T(8,128)} async-done(((f32[8,4096]{1,0:T(8,128)}), f32[8,4096]{1,0:T(8,128)}) %all-reduce.6.cloned.1.call-update) | async-done | bytes 131088 | tf_op jit(solution)/shard_map/psum | solution.py:80
  261.9 1.3 convolution_bitcast_fusion.5
  264.1 3.8 collective-permute-start
  267.9 1.3 collective-permute-start.1
  269.2 19.7 %reshape.113 = bf16[1,1,8,13,36864]{4,3,2,1,0:T(8,128)(2,1)} reshape(bf16[8,13,3,64,3,64]{5,4,3,2,1,0:T(4,128)(2,1)} %mul.97) | data formatting | bytes 15335424 | tf_op jit(solution)/shard_map/mul | solution.py:39
  289.1 3.5 collective-permute-start.2
  292.6 1.9 collective-permute-start.3
  294.6 8.0 collective-permute-done.3
  302.6 1.4 gather_fusion
  304.0 5.4 fusion.21
  311.2 4.8 collective-permute-start.4
  316.0 1.5 collective-permute-start.5
  317.5 11.9 %convert_reduce_fusion.1 = f32[8,36864]{1,0:T(8,128)} fusion(bf16[1,1,8,13,36864]{4,2,3,1,0:T(8,128)(2,1)} %param.11, bf16[1,1,8,13,36864]{4,3,2,1,0:T(8,128)(2,1)} %reshape.113), kind=kLoop, calls=%fused_computation.3 | loop fusion | flops 11206656 | bytes 16515072 | tf_op jit(solution)/shard_map/reduce_sum | solution.py:54
  329.4 2.0 reduce_sum.63
  331.4 2.9 reshape_squeeze.10
  337.2 2.1 collective-permute-start.6
  339.3 2.2 collective-permute-start.7
  341.5 6.7 fusion.35
  348.2 3.0 collective-permute-done.7
  351.2 1.3 multiply_reduce_fusion.2
  352.5 81.6 %all-reduce.2 = (f32[8]{0:T(128)S(1)}, f32[8]{0:T(128)S(1)}) all-reduce(f32[8]{0:T(128)S(1)} %get-tuple-element.4, f32[8]{0:T(128)S(1)} %get-tuple-element.3), channel_id=1, replica_groups=mesh['gx'=16,'gy'=16] {'gx','gy'}, use_global_device_ids=true, to_apply=%region_2.0 | all-reduce | flops 16 | bytes 128 | tf_op jit(solution)/shard_map/psum | solution.py:82
  435.4 1.4 fusion.81
  436.7 240.2 %all-reduce.8.cloned.1.call-done = f32[8,4096]{1,0:T(8,128)} async-done(((f32[8,4096]{1,0:T(8,128)}), f32[8,4096]{1,0:T(8,128)}) %all-reduce.8.cloned.1.call-update) | async-done | bytes 131088 | tf_op jit(solution)/shard_map/psum | solution.py:80
  676.9 1.3 convolution_bitcast_fusion.4
  678.6 76.3 %psum.46 = f32[8]{0:T(128)S(1)} all-reduce(f32[8]{0:T(128)S(1)} %get-tuple-element.24), channel_id=1, replica_groups=mesh['gx'=16,'gy'=16] {'gx','gy'}, use_global_device_ids=true, to_apply=%region_10.12 | all-reduce | flops 8 | bytes 64 | tf_op jit(solution)/shard_map/psum | solution.py:82
  755.0 2.4 collective-permute-start.8
  757.4 1.3 collective-permute-start.9
  758.7 3.7 collective-permute-done.9
  762.4 6.5 collective-permute-start.10
  768.9 1.9 collective-permute-start.11
  770.8 8.0 collective-permute-done.11
  779.5 4.8 fusion.18
  785.4 2.4 collective-permute-start.12
  787.7 1.3 collective-permute-start.13
  789.3 3.7 collective-permute-done.13
  793.2 4.2 collective-permute-start.14
  797.4 1.9 collective-permute-start.15
  799.3 5.5 fusion.32
  804.8 4.5 collective-permute-done.15
  809.7 79.3 %psum.47 = f32[8]{0:T(128)S(1)} all-reduce(f32[8]{0:T(128)S(1)} %get-tuple-element.7), channel_id=1, replica_groups=mesh['gx'=16,'gy'=16] {'gx','gy'}, use_global_device_ids=true, to_apply=%region_12.14 | all-reduce | flops 8 | bytes 64 | tf_op jit(solution)/shard_map/psum | solution.py:124
  (81 shorter events, 13.4 us)
Async XLA Ops:
  7.2 1.3 copy-start
  7.2 254.7 %all-reduce.6.cloned.1.call-start = ((), (), s32[]{:S(2)}) async-start(), calls=%async_computation | async-start | bytes 262144 | tf_op jit(solution)/shard_map/psum | solution.py:80
  9.4 667.5 %all-reduce.8.cloned.1.call-start = ((), (), s32[]{:S(2)}) async-start(), calls=%async_computation.1 | async-start | bytes 262144 | tf_op jit(solution)/shard_map/psum | solution.py:80
  79.0 14.1 %copy-start.11 = (s32[1,1,8,13]{3,2,1,0:T(8,128)S(1)}, s32[1,1,8,13]{3,2,1,0:T(8,128)}, u32[]{:S(2)}) copy-start(s32[1,1,8,13]{3,2,1,0:T(8,128)} %param.13) | copy-start | bytes 1252
  79.0 184.2 %copy-start.2 = (f32[1,1,16,8,192]{4,3,2,1,0:T(8,128)S(1)}, f32[1,1,16,8,192]{4,3,2,1,0:T(8,128)}, u32[]{:S(2)}) copy-start(f32[1,1,16,8,192]{4,3,2,1,0:T(8,128)} %param.16) | copy-start | bytes 294916
  79.0 184.2 %copy-start.10 = (f32[8,8,192]{2,1,0:T(8,128)S(1)}, f32[8,8,192]{2,1,0:T(8,128)}, u32[]{:S(2)}) copy-start(f32[8,8,192]{2,1,0:T(8,128)} %fusion.63) | copy-start | bytes 147460
  264.1 39.9 %copy-start.8 = (bf16[8,8,192]{2,1,0:T(8,128)(2,1)}, bf16[8,8,192]{2,1,0:T(8,128)(2,1)S(1)}, u32[]{:S(2)}) copy-start(bf16[8,8,192]{2,1,0:T(8,128)(2,1)S(1)} %get-tuple-element.22) | copy-start | bytes 73732
  264.1 25.0 %collective-permute-start = (bf16[1,1,8,8,192]{4,3,2,1,0:T(8,128)(2,1)S(1)}, bf16[1,1,8,8,192]{4,3,2,1,0:T(8,128)(2,1)S(1)}, u32[]{:S(2)}, u32[]{:S(2)}) collective-permute-start(bf16[1,1,8,8,192]{4,3,2,1,0:T(8,128)(2,1)S(1)} %bitcast.127), channel_id=1, source_target_pairs={{0,16},{16,32},{32,48},{48,64},{64,80},{80,96},{96,112},{112,128},... | collective-permute-start | bytes 73736 | tf_op jit(solution)/shard_map/ppermute | solution.py:23
  267.9 21.2 %collective-permute-start.1 = (bf16[1,1,8,8,192]{4,3,2,1,0:T(8,128)(2,1)S(1)}, bf16[1,1,8,8,192]{4,3,2,1,0:T(8,128)(2,1)S(1)}, u32[]{:S(2)}, u32[]{:S(2)}) collective-permute-start(bf16[1,1,8,8,192]{4,3,2,1,0:T(8,128)(2,1)S(1)} %bitcast.128), channel_id=1, source_target_pairs={{16,0},{32,16},{48,32},{64,48},{80,64},{96,80},{112,96},{128,112},... | collective-permute-start | bytes 73736 | tf_op jit(solution)/shard_map/ppermute | solution.py:24
  289.0 15.0 %copy-start.4 = (f32[8,13,192]{2,1,0:T(8,128)}, f32[8,13,192]{2,1,0:T(8,128)S(1)}, u32[]{:S(2)}) copy-start(f32[8,13,192]{2,1,0:T(8,128)S(1)} %copy.49) | copy-start | bytes 239620
  289.1 5.5 collective-permute-start.2
  292.6 9.9 %collective-permute-start.3 = (bf16[3,1,8,8,192]{4,3,2,1,0:T(8,128)(2,1)S(1)}, bf16[3,1,8,8,192]{4,3,2,1,0:T(8,128)(2,1)S(1)}, u32[]{:S(2)}, u32[]{:S(2)}) collective-permute-start(bf16[3,1,8,8,192]{4,3,2,1,0:T(8,128)(2,1)S(1)} %pad_maximum_fusion.6), channel_id=1, source_target_pairs={{1,0},{2,1},{3,2},{4,3},{5,4},{6,5},{7,6},{8,7},{9,8},{10,9},{11,1... | collective-permute-start | bytes 221192 | tf_op jit(solution)/shard_map/ppermute | solution.py:24
  310.5 7.0 copy-start.3
  311.2 25.0 %collective-permute-start.4 = (bf16[1,3,8,8,192]{4,3,2,1,0:T(8,128)(2,1)}, bf16[1,3,8,8,192]{4,3,2,1,0:T(8,128)(2,1)}, u32[]{:S(2)}, u32[]{:S(2)}) collective-permute-start(bf16[1,3,8,8,192]{4,3,2,1,0:T(8,128)(2,1)} %get-tuple-element.18), channel_id=1, source_target_pairs={{0,16},{16,32},{32,48},{48,64},{64,80},{80,96},{96,112},{112,128},... | collective-permute-start | bytes 221192 | tf_op jit(solution)/shard_map/ppermute | solution.py:23
  316.0 20.3 %collective-permute-start.5 = (bf16[1,3,8,8,192]{4,3,2,1,0:T(8,128)(2,1)}, bf16[1,3,8,8,192]{4,3,2,1,0:T(8,128)(2,1)}, u32[]{:S(2)}, u32[]{:S(2)}) collective-permute-start(bf16[1,3,8,8,192]{4,3,2,1,0:T(8,128)(2,1)} %get-tuple-element.19), channel_id=1, source_target_pairs={{16,0},{32,16},{48,32},{64,48},{80,64},{96,80},{112,96},{128,112},... | collective-permute-start | bytes 221192 | tf_op jit(solution)/shard_map/ppermute | solution.py:24
  335.2 16.0 %copy-start.1 = (bf16[8,192,192]{2,1,0:T(8,128)(2,1)S(1)}, bf16[8,192,192]{2,1,0:T(8,128)(2,1)}, u32[]{:S(2)}) copy-start(bf16[8,192,192]{2,1,0:T(8,128)(2,1)} %reshape_squeeze.10) | copy-start | bytes 1769476
  335.2 16.0 %copy-start.6 = (f32[8,8,192]{2,1,0:T(8,128)S(1)}, f32[8,8,192]{2,1,0:T(8,128)}, u32[]{:S(2)}) copy-start(f32[8,8,192]{2,1,0:T(8,128)} %get-tuple-element.23) | copy-start | bytes 147460
  335.2 16.0 %copy-start.7 = (f32[1,1,8,8,192]{4,3,2,1,0:T(8,128)S(1)}, f32[1,1,8,8,192]{4,3,2,1,0:T(8,128)}, u32[]{:S(2)}) copy-start(f32[1,1,8,8,192]{4,3,2,1,0:T(8,128)} %param.10) | copy-start | bytes 147460
  335.2 16.0 %copy-start.9 = (bf16[8,8,192]{2,1,0:T(8,128)(2,1)S(1)}, bf16[8,8,192]{2,1,0:T(8,128)(2,1)}, u32[]{:S(2)}) copy-start(bf16[8,8,192]{2,1,0:T(8,128)(2,1)} %copy-done.8) | copy-start | bytes 73732
  335.2 444.3 %copy-start.5 = (f32[8,13,192]{2,1,0:T(8,128)S(1)}, f32[8,13,192]{2,1,0:T(8,128)}, u32[]{:S(2)}) copy-start(f32[8,13,192]{2,1,0:T(8,128)} %copy-done.4) | copy-start | bytes 239620
  337.2 11.0 %collective-permute-start.6 = (bf16[5,1,8,8,192]{4,3,2,1,0:T(8,128)(2,1)S(1)}, bf16[5,1,8,8,192]{4,3,2,1,0:T(8,128)(2,1)S(1)}, u32[]{:S(2)}, u32[]{:S(2)}) collective-permute-start(bf16[5,1,8,8,192]{4,3,2,1,0:T(8,128)(2,1)S(1)} %get-tuple-element.14), channel_id=1, source_target_pairs={{0,1},{1,2},{2,3},{3,4},{4,5},{5,6},{6,7},{7,8},{8,9},{9,10},{10,1... | collective-permute-start | bytes 368648 | tf_op jit(solution)/shard_map/ppermute | solution.py:23
  339.3 11.9 %collective-permute-start.7 = (bf16[5,1,8,8,192]{4,3,2,1,0:T(8,128)(2,1)S(1)}, bf16[5,1,8,8,192]{4,3,2,1,0:T(8,128)(2,1)S(1)}, u32[]{:S(2)}, u32[]{:S(2)}) collective-permute-start(bf16[5,1,8,8,192]{4,3,2,1,0:T(8,128)(2,1)S(1)} %get-tuple-element.15), channel_id=1, source_target_pairs={{1,0},{2,1},{3,2},{4,3},{5,4},{6,5},{7,6},{8,7},{9,8},{10,9},{11,1... | collective-permute-start | bytes 368648 | tf_op jit(solution)/shard_map/ppermute | solution.py:24
  678.2 121.1 %copy-start.12 = (f32[8,192]{1,0:T(8,128)S(1)}, f32[8,192]{1,0:T(8,128)}, u32[]{:S(2)}) copy-start(f32[8,192]{1,0:T(8,128)} %reduce_sum.64) | copy-start | bytes 18436
  755.0 3.7 collective-permute-start.8
  757.4 5.0 collective-permute-start.9
  762.4 8.4 collective-permute-start.10
  768.9 9.9 %collective-permute-start.11 = (bf16[3,1,8,8,192]{4,3,2,1,0:T(8,128)(2,1)S(1)}, bf16[3,1,8,8,192]{4,3,2,1,0:T(8,128)(2,1)S(1)}, u32[]{:S(2)}, u32[]{:S(2)}) collective-permute-start(bf16[3,1,8,8,192]{4,3,2,1,0:T(8,128)(2,1)S(1)} %pad_maximum_fusion.7), channel_id=1, source_target_pairs={{1,0},{2,1},{3,2},{4,3},{5,4},{6,5},{7,6},{8,7},{9,8},{10,9},{11,1... | collective-permute-start | bytes 221192 | tf_op jit(solution)/shard_map/ppermute | solution.py:24
  785.4 4.0 collective-permute-start.12
  787.7 5.4 collective-permute-start.13
  793.2 11.6 %collective-permute-start.14 = (bf16[5,1,8,8,192]{4,3,2,1,0:T(8,128)(2,1)S(1)}, bf16[5,1,8,8,192]{4,3,2,1,0:T(8,128)(2,1)S(1)}, u32[]{:S(2)}, u32[]{:S(2)}) collective-permute-start(bf16[5,1,8,8,192]{4,3,2,1,0:T(8,128)(2,1)S(1)} %get-tuple-element.12), channel_id=1, source_target_pairs={{0,1},{1,2},{2,3},{3,4},{4,5},{5,6},{6,7},{7,8},{8,9},{9,10},{10,1... | collective-permute-start | bytes 368648 | tf_op jit(solution)/shard_map/ppermute | solution.py:23
  797.4 11.9 %collective-permute-start.15 = (bf16[5,1,8,8,192]{4,3,2,1,0:T(8,128)(2,1)S(1)}, bf16[5,1,8,8,192]{4,3,2,1,0:T(8,128)(2,1)S(1)}, u32[]{:S(2)}, u32[]{:S(2)}) collective-permute-start(bf16[5,1,8,8,192]{4,3,2,1,0:T(8,128)(2,1)S(1)} %get-tuple-element.13), channel_id=1, source_target_pairs={{1,0},{2,1},{3,2},{4,3},{5,4},{6,5},{7,6},{8,7},{9,8},{10,9},{11,1... | collective-permute-start | bytes 368648 | tf_op jit(solution)/shard_map/ppermute | solution.py:24
Sparse Core Ops, SparseCore 0:
  13.5 248.3 all-reduce.5
  435.5 241.3 all-reduce.7
where the time goes:
time: 899 us; the launch traced here: 897 us
  waiting for transfers between devices  440 us (49%)
  blocking collectives  237 us (26%)
  local copies, waits for them, and re-layouts  94.9 us (11%)
  starting transfers between devices  43 us (5%)
  matrix products  36.3 us (4%)
  other arithmetic  30.5 us (3%)
  between operations  14.5 us (2%)
    psum x2, waiting for transfers between devices, precondition(): summed = lax.psum(coarse_term, ('gx', 'gy'))  409 us
    psum x2, blocking collectives, precondition(): energy = lax.psum(jnp.sum(residual * smoothed, axis=(0, 2)), ('gx', 'gy'))  158 us
    psum x1, blocking collectives, per_device(): lax.psum(jnp.sum(direction * operator_out, axis=(0, 2)), ('gx', 'gy'))  79.3 us
    mul x3, local copies, waits for them, and re-layouts, masked_blocks(): masked = shaped * intact[..., None, :, None, :]  63.1 us
    ppermute x8, waiting for transfers between devices, padded_2(): after = lax.ppermute(initial, axis, down)  30.9 us
    ppermute x8, starting transfers between devices, padded_2(): before = lax.ppermute(last, axis, up)  29.6 us
  transfers between devices with their start and end apart: 18, of which 9 were waited for; matrix products, arithmetic and copies ran while one was open for 15% of the time, Pallas kernels for 0%

commit v1 on v0

--- a/solution.py
+++ b/solution.py
@@ -77,7 +77,7 @@
     def precondition(residual):
         own_part = smooth_local(residual)
         coarse_term = restrict(residual)
-        summed = lax.psum(coarse_term, ("gx", "gy"))
+        summed = jnp.sum(lax.all_gather(coarse_term, ("gx", "gy")), axis=0)
         smoothed = own_part + prolong(summed)
         energy = lax.psum(jnp.sum(residual * smoothed, axis=(0, 2)), ("gx", "gy"))
         return (smoothed, energy)

time: 899 us -> 1310 us (1.46)
  waiting for transfers between devices: 440 us -> 809 us
  other arithmetic: 30.5 us -> 54.6 us
  starting transfers between devices: 43 us -> 64.3 us
    all_gather x0 -> x2, waiting for transfers between devices: none -> 803 us  [precondition(): summed = jnp.sum(lax.all_gather(coarse_term, ('gx', 'gy')), axis=0)]
    psum x2 -> x0, waiting for transfers between devices: 409 us -> none  [precondition(): summed = lax.psum(coarse_term, ('gx', 'gy'))]
    ppermute x8, waiting for transfers between devices: 30.9 us -> 0.86 us  [padded_2(): after = lax.ppermute(initial, axis, down)]
    reduce_sum x0 -> x2, other arithmetic: none -> 24.1 us  [precondition(): summed = jnp.sum(lax.all_gather(coarse_term, ('gx', 'gy')), axis=0)]
    ppermute x8, starting transfers between devices: 29.6 us -> 45.9 us  [padded_2(): before = lax.ppermute(last, axis, up)]
  transfers between devices with their start and end apart: 18 -> 18, of which waited for: 9 -> 8; matrix products, arithmetic and copies ran while one was open for 15% -> 10% of each run, Pallas kernels for 0% -> 0%
where the time goes in v1:
time: 1310 us
  waiting for transfers between devices  809 us (62%)
  blocking collectives  238 us (18%)
  local copies, waits for them, and re-layouts  95.2 us (7%)
  starting transfers between devices  64.3 us (5%)
  other arithmetic  54.6 us (4%)
  matrix products  33 us (3%)
  between operations  14.5 us (1%)
    all_gather x2, waiting for transfers between devices, precondition(): summed = jnp.sum(lax.all_gather(coarse_term, ('gx', 'gy')), axis=0)  803 us
    psum x2, blocking collectives, precondition(): energy = lax.psum(jnp.sum(residual * smoothed, axis=(0, 2)), ('gx', 'gy'))  155 us
    psum x1, blocking collectives, per_device(): lax.psum(jnp.sum(direction * operator_out, axis=(0, 2)), ('gx', 'gy'))  83 us
    mul x3, local copies, waits for them, and re-layouts, masked_blocks(): masked = shaped * intact[..., None, :, None, :]  63.4 us
    ppermute x8, starting transfers between devices, padded_2(): before = lax.ppermute(last, axis, up)  45.9 us
  transfers between devices with their start and end apart: 18, of which 8 were waited for; matrix products, arithmetic and copies ran while one was open for 10% of the time, Pallas kernels for 0%

profile of v1, /device:TPU:1, one launch (start us, length us, event | category | flops | bytes accessed | tf_op | source)
XLA Modules:
  0.0 1308.6 jit_solution(5038043465383825100)
XLA Ops:
  7.2 1.2 convolution_bitcast_fusion.3
  9.5 2.0 reshape_squeeze.9
  11.5 16.6 %reshape_squeeze.11 = bf16[8,13,192,192]{3,2,0,1:T(8,128)(2,1)} reshape(bf16[1,1,8,13,36864]{4,2,3,1,0:T(8,128)(2,1)} %param.11) | data formatting | bytes 15335424 | tf_op jit(solution)/shard_map/reshape;squeeze | solution.py:38
  28.2 1.5 fusion.9
  29.7 3.0 copy.45
  32.7 8.9 mul.97
  41.6 34.8 %mul.102 = bf16[8,13,192,192]{3,2,1,0:T(8,128)(2,1)} reshape(bf16[8,13,3,64,3,64]{5,4,3,2,1,0:T(4,128)(2,1)} %mul.97) | data formatting | bytes 15335424 | tf_op jit(solution)/shard_map/mul | solution.py:39
  76.4 1.4 fusion.63
  77.8 14.1 %convert_reduce_fusion = (f32[8,13,192]{2,0,1:T(8,128)S(1)}, bf16[8,13,192,192]{3,2,0,1:T(8,128)(2,1)}) fusion(bf16[8,13,192,192]{3,2,0,1:T(8,128)(2,1)} %reshape_squeeze.11, bf16[8,13,192,192]{3,2,1,0:T(8,128)(2,1)} %mul.102), kind=kLoop, calls=%fused_computation.4 | loop fusion | flops 11481600 | bytes 23083008 | tf_op jit(solution)/shard_map/reduce_sum | solution.py:55
  91.9 365.9 %all-gather.5.cloned.1.call-done = f32[2048,4096]{1,0:T(8,128)} async-done(((f32[8,4096]{1,0:T(8,128)}), f32[2048,4096]{1,0:T(8,128)}) %all-gather.5.cloned.1.call-update) | async-done | bytes 33554448 | tf_op jit(solution)/shard_map/all_gather | solution.py:80
  457.8 12.1 bitcast_reduce_fusion.1
  471.1 1.3 collective-permute-start.1
  472.4 4.0 collective-permute-start
  476.5 19.7 %reshape.115 = bf16[1,1,8,13,36864]{4,3,2,1,0:T(8,128)(2,1)} reshape(bf16[8,13,3,64,3,64]{5,4,3,2,1,0:T(4,128)(2,1)} %mul.97) | data formatting | bytes 15335424 | tf_op jit(solution)/shard_map/mul | solution.py:39
  496.4 5.6 collective-permute-start.3
  502.0 5.3 collective-permute-start.2
  507.6 1.3 collective-permute-done.2
  508.9 1.4 gather_fusion
  510.3 5.4 fusion.21
  517.5 1.3 collective-permute-start.5
  518.8 4.6 collective-permute-start.4
  523.4 11.9 convert_reduce_fusion.1
  535.3 2.0 reduce_sum.82
  537.3 2.9 reshape_squeeze.10
  541.1 1.1 slice.123
  543.1 1.9 collective-permute-start.7
  545.0 8.8 collective-permute-start.6
  553.8 6.7 fusion.35
  560.5 1.3 multiply_reduce_fusion.2
  561.8 80.1 %all-reduce.2 = (f32[8]{0:T(128)S(1)}, f32[8]{0:T(128)S(1)}) all-reduce(f32[8]{0:T(128)S(1)} %get-tuple-element.4, f32[8]{0:T(128)S(1)} %get-tuple-element.3), channel_id=1, replica_groups=mesh['gx'=16,'gy'=16] {'gx','gy'}, use_global_device_ids=true, to_apply=%region_2.0 | all-reduce | flops 16 | bytes 128 | tf_op jit(solution)/shard_map/psum | solution.py:82
  643.2 1.4 fusion.81
  644.6 437.4 %all-gather.7.cloned.1.call-done = f32[2048,4096]{1,0:T(8,128)} async-done(((f32[8,4096]{1,0:T(8,128)}), f32[2048,4096]{1,0:T(8,128)}) %all-gather.7.cloned.1.call-update) | async-done | bytes 33554448 | tf_op jit(solution)/shard_map/all_gather | solution.py:80
  1082.0 12.1 bitcast_reduce_fusion
  1094.8 74.6 %psum.30 = f32[8]{0:T(128)S(1)} all-reduce(f32[8]{0:T(128)S(1)} %get-tuple-element.24), channel_id=1, replica_groups=mesh['gx'=16,'gy'=16] {'gx','gy'}, use_global_device_ids=true, to_apply=%region_10.12 | all-reduce | flops 8 | bytes 64 | tf_op jit(solution)/shard_map/psum | solution.py:82
  1169.5 1.3 collective-permute-start.9
  1170.8 4.0 collective-permute-start.8
  1174.8 1.0 collective-permute-done.8
  1175.8 3.7 collective-permute-start.11
  1179.5 5.8 collective-permute-start.10
  1185.8 1.3 collective-permute-done.10
  1187.7 4.8 fusion.18
  1193.6 1.3 collective-permute-start.13
  1194.9 4.2 collective-permute-start.12
  1199.1 1.6 collective-permute-done.12
  1200.8 1.9 collective-permute-start.15
  1202.7 9.4 collective-permute-start.14
  1212.1 5.5 fusion.32
  1218.0 83.0 %psum.31 = f32[8]{0:T(128)S(1)} all-reduce(f32[8]{0:T(128)S(1)} %get-tuple-element.7), channel_id=1, replica_groups=mesh['gx'=16,'gy'=16] {'gx','gy'}, use_global_device_ids=true, to_apply=%region_12.14 | all-reduce | flops 8 | bytes 64 | tf_op jit(solution)/shard_map/psum | solution.py:124
  (83 shorter events, 12.4 us)
Async XLA Ops:
  7.2 1.3 copy-start
  7.2 450.6 %all-gather.5.cloned.1.call-start = ((), (), s32[]{:S(2)}) async-start(), calls=%async_computation | async-start | bytes 33685504 | tf_op jit(solution)/shard_map/all_gather | solution.py:80
  9.4 1072.5 %all-gather.7.cloned.1.call-start = ((), (), s32[]{:S(2)}) async-start(), calls=%async_computation.1 | async-start | bytes 33685504 | tf_op jit(solution)/shard_map/all_gather | solution.py:80
  41.6 34.8 %copy-start.11 = (s32[1,1,8,13]{3,2,1,0:T(8,128)S(1)}, s32[1,1,8,13]{3,2,1,0:T(8,128)}, u32[]{:S(2)}) copy-start(s32[1,1,8,13]{3,2,1,0:T(8,128)} %param.13) | copy-start | bytes 1252
  41.6 34.8 %copy-start.7 = (f32[1,1,8,8,192]{4,3,2,1,0:T(8,128)S(1)}, f32[1,1,8,8,192]{4,3,2,1,0:T(8,128)}, u32[]{:S(2)}) copy-start(f32[1,1,8,8,192]{4,3,2,1,0:T(8,128)} %param.10) | copy-start | bytes 147460
  91.9 378.3 %copy-start.2 = (f32[1,1,16,8,192]{4,3,2,1,0:T(8,128)S(1)}, f32[1,1,16,8,192]{4,3,2,1,0:T(8,128)}, u32[]{:S(2)}) copy-start(f32[1,1,16,8,192]{4,3,2,1,0:T(8,128)} %param.16) | copy-start | bytes 294916
  471.1 39.2 %copy-start.9 = (bf16[8,8,192]{2,1,0:T(8,128)(2,1)}, bf16[8,8,192]{2,1,0:T(8,128)(2,1)S(1)}, u32[]{:S(2)}) copy-start(bf16[8,8,192]{2,1,0:T(8,128)(2,1)S(1)} %get-tuple-element.22) | copy-start | bytes 73732
  471.1 25.2 %collective-permute-start.1 = (bf16[1,1,8,8,192]{4,3,2,1,0:T(8,128)(2,1)S(1)}, bf16[1,1,8,8,192]{4,3,2,1,0:T(8,128)(2,1)S(1)}, u32[]{:S(2)}, u32[]{:S(2)}) collective-permute-start(bf16[1,1,8,8,192]{4,3,2,1,0:T(8,128)(2,1)S(1)} %bitcast.131), channel_id=1, source_target_pairs={{16,0},{32,16},{48,32},{64,48},{80,64},{96,80},{112,96},{128,112},... | collective-permute-start | bytes 73736 | tf_op jit(solution)/shard_map/ppermute | solution.py:24
  472.4 23.9 %collective-permute-start = (bf16[1,1,8,8,192]{4,3,2,1,0:T(8,128)(2,1)S(1)}, bf16[1,1,8,8,192]{4,3,2,1,0:T(8,128)(2,1)S(1)}, u32[]{:S(2)}, u32[]{:S(2)}) collective-permute-start(bf16[1,1,8,8,192]{4,3,2,1,0:T(8,128)(2,1)S(1)} %bitcast.132), channel_id=1, source_target_pairs={{0,16},{16,32},{32,48},{48,64},{64,80},{80,96},{96,112},{112,128},... | collective-permute-start | bytes 73736 | tf_op jit(solution)/shard_map/ppermute | solution.py:23
  496.3 14.1 %copy-start.4 = (f32[8,13,192]{2,1,0:T(8,128)}, f32[8,13,192]{2,1,0:T(8,128)S(1)}, u32[]{:S(2)}) copy-start(f32[8,13,192]{2,1,0:T(8,128)S(1)} %copy.49) | copy-start | bytes 239620
  496.4 11.2 collective-permute-start.3
  502.0 6.9 collective-permute-start.2
  516.8 6.7 copy-start.3
  517.5 24.7 %collective-permute-start.5 = (bf16[1,3,8,8,192]{4,3,2,1,0:T(8,128)(2,1)}, bf16[1,3,8,8,192]{4,3,2,1,0:T(8,128)(2,1)}, u32[]{:S(2)}, u32[]{:S(2)}) collective-permute-start(bf16[1,3,8,8,192]{4,3,2,1,0:T(8,128)(2,1)} %get-tuple-element.19), channel_id=1, source_target_pairs={{16,0},{32,16},{48,32},{64,48},{80,64},{96,80},{112,96},{128,112},... | collective-permute-start | bytes 221192 | tf_op jit(solution)/shard_map/ppermute | solution.py:24
  518.8 23.4 %collective-permute-start.4 = (bf16[1,3,8,8,192]{4,3,2,1,0:T(8,128)(2,1)}, bf16[1,3,8,8,192]{4,3,2,1,0:T(8,128)(2,1)}, u32[]{:S(2)}, u32[]{:S(2)}) collective-permute-start(bf16[1,3,8,8,192]{4,3,2,1,0:T(8,128)(2,1)} %get-tuple-element.18), channel_id=1, source_target_pairs={{0,16},{16,32},{32,48},{48,64},{64,80},{80,96},{96,112},{112,128},... | collective-permute-start | bytes 221192 | tf_op jit(solution)/shard_map/ppermute | solution.py:23
  541.1 19.4 %copy-start.1 = (bf16[8,192,192]{2,1,0:T(8,128)(2,1)S(1)}, bf16[8,192,192]{2,1,0:T(8,128)(2,1)}, u32[]{:S(2)}) copy-start(bf16[8,192,192]{2,1,0:T(8,128)(2,1)} %reshape_squeeze.10) | copy-start | bytes 1769476
  541.1 19.4 %copy-start.6 = (f32[8,8,192]{2,1,0:T(8,128)S(1)}, f32[8,8,192]{2,1,0:T(8,128)}, u32[]{:S(2)}) copy-start(f32[8,8,192]{2,1,0:T(8,128)} %get-tuple-element.23) | copy-start | bytes 147460
  541.1 19.4 %copy-start.8 = (f32[1,1,8,8,192]{4,3,2,1,0:T(8,128)S(1)}, f32[1,1,8,8,192]{4,3,2,1,0:T(8,128)}, u32[]{:S(2)}) copy-start(f32[1,1,8,8,192]{4,3,2,1,0:T(8,128)} %param.10) | copy-start | bytes 147460
  541.1 19.4 %copy-start.10 = (bf16[8,8,192]{2,1,0:T(8,128)(2,1)S(1)}, bf16[8,8,192]{2,1,0:T(8,128)(2,1)}, u32[]{:S(2)}) copy-start(bf16[8,8,192]{2,1,0:T(8,128)(2,1)} %copy-done.9) | copy-start | bytes 73732
  543.1 17.4 %collective-permute-start.7 = (bf16[5,1,8,8,192]{4,3,2,1,0:T(8,128)(2,1)S(1)}, bf16[5,1,8,8,192]{4,3,2,1,0:T(8,128)(2,1)S(1)}, u32[]{:S(2)}, u32[]{:S(2)}) collective-permute-start(bf16[5,1,8,8,192]{4,3,2,1,0:T(8,128)(2,1)S(1)} %get-tuple-element.15), channel_id=1, source_target_pairs={{1,0},{2,1},{3,2},{4,3},{5,4},{6,5},{7,6},{8,7},{9,8},{10,9},{11,1... | collective-permute-start | bytes 368648 | tf_op jit(solution)/shard_map/ppermute | solution.py:24
  545.0 15.5 %collective-permute-start.6 = (bf16[5,1,8,8,192]{4,3,2,1,0:T(8,128)(2,1)S(1)}, bf16[5,1,8,8,192]{4,3,2,1,0:T(8,128)(2,1)S(1)}, u32[]{:S(2)}, u32[]{:S(2)}) collective-permute-start(bf16[5,1,8,8,192]{4,3,2,1,0:T(8,128)(2,1)S(1)} %get-tuple-element.14), channel_id=1, source_target_pairs={{0,1},{1,2},{2,3},{3,4},{4,5},{5,6},{6,7},{7,8},{8,9},{9,10},{10,1... | collective-permute-start | bytes 368648 | tf_op jit(solution)/shard_map/ppermute | solution.py:23
  644.6 543.1 %copy-start.5 = (f32[8,13,192]{2,1,0:T(8,128)S(1)}, f32[8,13,192]{2,1,0:T(8,128)}, u32[]{:S(2)}) copy-start(f32[8,13,192]{2,1,0:T(8,128)} %copy-done.4) | copy-start | bytes 239620
  1094.4 117.7 %copy-start.12 = (f32[8,192]{1,0:T(8,128)S(1)}, f32[8,192]{1,0:T(8,128)}, u32[]{:S(2)}) copy-start(f32[8,192]{1,0:T(8,128)} %reduce_sum.83) | copy-start | bytes 18436
  1169.5 5.3 collective-permute-start.9
  1170.8 5.0 collective-permute-start.8
  1175.8 9.9 collective-permute-start.11
  1179.5 7.5 collective-permute-start.10
  1193.6 5.5 collective-permute-start.13
  1194.9 5.8 collective-permute-start.12
  1200.8 16.8 %collective-permute-start.15 = (bf16[5,1,8,8,192]{4,3,2,1,0:T(8,128)(2,1)S(1)}, bf16[5,1,8,8,192]{4,3,2,1,0:T(8,128)(2,1)S(1)}, u32[]{:S(2)}, u32[]{:S(2)}) collective-permute-start(bf16[5,1,8,8,192]{4,3,2,1,0:T(8,128)(2,1)S(1)} %get-tuple-element.13), channel_id=1, source_target_pairs={{1,0},{2,1},{3,2},{4,3},{5,4},{6,5},{7,6},{8,7},{9,8},{10,9},{11,1... | collective-permute-start | bytes 368648 | tf_op jit(solution)/shard_map/ppermute | solution.py:24
  1202.7 14.9 %collective-permute-start.14 = (bf16[5,1,8,8,192]{4,3,2,1,0:T(8,128)(2,1)S(1)}, bf16[5,1,8,8,192]{4,3,2,1,0:T(8,128)(2,1)S(1)}, u32[]{:S(2)}, u32[]{:S(2)}) collective-permute-start(bf16[5,1,8,8,192]{4,3,2,1,0:T(8,128)(2,1)S(1)} %get-tuple-element.12), channel_id=1, source_target_pairs={{0,1},{1,2},{2,3},{3,4},{4,5},{5,6},{6,7},{7,8},{8,9},{9,10},{10,1... | collective-permute-start | bytes 368648 | tf_op jit(solution)/shard_map/ppermute | solution.py:23
Sparse Core Ops, SparseCore 0:
  9.9 447.8 all-gather.4
  643.4 438.5 all-gather.6
